TPU v7x, 32 devices: a whole 2x2x4 slice. The times are simulated.
32 devices in a mesh: swath: 2 (over y), sub: 4 (over z), beam: 2 (over x), half: 2 (over core).
Axes of the slice: x: 2, y: 2, z: 4, core: 2. Of those that a mesh axis runs over, the one named last changes fastest.
Arguments:
- images: bfloat16 [4, 2, 2048, 1024], P('sub', None, ('swath', 'half'), 'beam'), parts along dimension 2, may hold values from -6 to 6
- offsets: float32 [4], replicated, may hold values from 3840 to 4505
- owners: int32 [2, 4], replicated, may hold values from 0 to 3, each once within a row
Outputs:
- sectors: bfloat16 [8, 1, 2, 512, 2048], P(('sub', 'beam'), None, None, None, ('swath', 'half')), parts along dimension 4
There are 2 independent parts, one for each index of `swath`. A program takes and returns all parts, laid end to end along the dimension named above; an argument that names none is the same for every part. Nothing has to cross between parts.
Inputs may be any that keep to these rules, and one draw needn't show every extreme that they name: Each row of owners names every one of the 4 sectors of its beam shard exactly once.
All inputs are finite; a program needn't handle non-finite values.
Results may differ from a plain program's by a relative error of at most 0.0052.
Values may be sent and summed in bfloat16 or wider, within the bound.
No kernel may reach another device: no remote copies, remote signals or barrier semaphores. Data moves between devices by JAX's collectives and lax.ppermute only.
A program may use at most 64 MiB of HBM per device.

v0:
```python
import math
import jax
import jax.numpy as jnp
from jax import lax
from jax.sharding import PartitionSpec as P

B = 1024
NR = 1024


def swapped(value, axis, distance):
    return lax.ppermute(value, axis, [(i, i ^ 1 << distance) for i in range(lax.axis_size(axis))])


def odd_kernel(beam_total, columns):
    source_ix = lax.broadcasted_iota(jnp.int32, (beam_total, columns), 0)
    target_ix = lax.broadcasted_iota(jnp.int32, (beam_total, columns), 1)
    spacing = target_ix - source_ix
    parity = jnp.where(spacing % 2 == 0, 1.0, -1.0).astype(jnp.float32)
    angles = (2.0 * spacing.astype(jnp.float32) + 1.0) * (math.pi / (2.0 * beam_total))
    return (parity * jnp.cos(angles) / (beam_total * jnp.sin(angles))).astype(jnp.bfloat16)


def steer_phase(upsampled, shifts, rows_at, beams_at, beams_out):
    ratios = NR / (NR + rows_at.astype(jnp.float32))
    tilts = (2.0 * beams_at.astype(jnp.float32) + 1.0) / beams_out - 1.0
    phases = ratios[:, None] * tilts[None, :] * shifts[..., None, None]
    cosine = jnp.cos(phases)
    sines = jnp.sin(phases)
    real_part = upsampled[..., 0, :, :]
    imag_part = upsampled[..., 1, :, :]
    return jnp.stack(
        [real_part * cosine - imag_part * sines, real_part * sines + imag_part * cosine], -3
    )


def rotate_sum(children, odd_beams, shifts, rows_at, beams_out):
    count = children.shape[-1]
    even_at = 2 * jnp.arange(count, dtype=jnp.int32)
    even_sum = jnp.sum(
        steer_phase(children.astype(jnp.float32), shifts, rows_at, even_at, beams_out), axis=0
    )
    odd_sum = jnp.sum(steer_phase(odd_beams, shifts, rows_at, even_at + 1, beams_out), axis=0)
    joined = jnp.stack([even_sum, odd_sum], -1)
    return joined.reshape(even_sum.shape[:-1] + (2 * count,)).astype(jnp.bfloat16)


def odd_local(children, kernel):
    product = jnp.dot(
        children.reshape(-1, children.shape[-1]), kernel, preferred_element_type=jnp.float32
    )
    return product.reshape(children.shape[:-1] + (kernel.shape[1],))


def swap_first(pieces):
    return swapped(pieces, "sub", 0)


def swap_second(pieces):
    return swapped(pieces, "sub", 1)


def keep_and_trade(field, which_bit, swapper):
    length = field.shape[2] // 2
    kept = lax.dynamic_slice_in_dim(field, which_bit * length, length, 2)
    given = lax.dynamic_slice_in_dim(field, (1 - which_bit) * length, length, 2)
    return (jnp.stack([kept, swapper(given)]), length)


def shift_block(offsets, index, per_device):
    return lax.dynamic_slice_in_dim(offsets, index * per_device, per_device, 0)


def body(images, offsets, owners):
    sub_count = lax.axis_size("sub")
    beam_count = lax.axis_size("beam")
    sub_place = lax.axis_index("sub")
    beam_lane = lax.axis_index("beam")
    half_side = lax.axis_index("half")
    low_bit = sub_place % 2
    high_bit = sub_place // 2 % 2
    per_device = images.shape[0]
    half_rows = images.shape[2]
    own_shift = shift_block(offsets, sub_place, per_device)
    mate_shift = shift_block(offsets, jnp.bitwise_xor(sub_place, 1), per_device)
    shifts_one = jnp.stack([own_shift, mate_shift])
    pair_base = sub_place - low_bit
    mate_base = jnp.bitwise_xor(sub_place, 2) - low_bit
    center_own = (
        shift_block(offsets, pair_base, per_device)
        + shift_block(offsets, pair_base + 1, per_device)
    ) * 0.5
    center_mate = (
        shift_block(offsets, mate_base, per_device)
        + shift_block(offsets, mate_base + 1, per_device)
    ) * 0.5
    shifts_two = jnp.stack([center_own, center_mate])
    all_beams = lax.all_to_all(images, "beam", split_axis=2, concat_axis=3, tiled=True)
    block_rows = all_beams.shape[2]
    start_row = half_side * half_rows + beam_lane * block_rows
    children, length = keep_and_trade(all_beams, low_bit, swap_first)
    rows_at = start_row + low_bit * length + jnp.arange(length, dtype=jnp.int32)
    odd_beams = odd_local(children, odd_kernel(B, B))
    first_merge = rotate_sum(children, odd_beams, shifts_one, rows_at, 2 * B)
    children, quarter = keep_and_trade(first_merge, high_bit, swap_second)
    rows_at = (
        start_row + low_bit * length + high_bit * quarter + jnp.arange(quarter, dtype=jnp.int32)
    )
    odd_beams = odd_local(children, odd_kernel(2 * B, 2 * B))
    merged = rotate_sum(children, odd_beams, shifts_two, rows_at, 4 * B)
    sector_tiles = merged.reshape(per_device, 2, quarter, beam_count, sub_count, -1)
    beam_ids = jnp.arange(beam_count, dtype=jnp.int32)[:, None]
    picked = sector_tiles[:, :, :, beam_ids, owners, :]
    outgoing = picked.transpose(4, 3, 0, 1, 5, 2)
    received = lax.all_to_all(
        lax.all_to_all(outgoing, "sub", split_axis=0, concat_axis=0, tiled=True),
        "beam",
        split_axis=1,
        concat_axis=1,
        tiled=True,
    )
    sector_width = received.shape[4]
    received = received.reshape(
        sub_count // 4, 2, 2, beam_count, per_device, 2, sector_width, quarter
    )
    received = received.transpose(0, 4, 5, 6, 3, 2, 1, 7)
    return received.reshape(1, sub_count // 4 * per_device, 2, sector_width, half_rows)


def solution(mesh):
    placed = (P("sub", None, ("swath", "half"), "beam"), P(), P())
    return jax.shard_map(
        body,
        mesh=mesh,
        in_specs=placed,
        out_specs=P(("sub", "beam"), None, None, None, ("swath", "half")),
        check_vma=False,
    )
```

profile of v0, /device:TPU:0, one launch (start us, length us, event | category | flops | bytes accessed | tf_op | source)
XLA Modules:
  0.0 222.6 jit_solution(12710477142224495665)
XLA Ops:
  0.0 3.3 %copy.32 = bf16[1,2,512,512]{3,1,0,2:T(2,128)(2,1)} copy(bf16[1,2,512,512]{3,2,1,0:T(8,128)(2,1)} %param.3) | data formatting | bytes 2097152 | tf_op args[0]
  3.3 4.2 %all-to-all-start = ((bf16[1,2,512,512]{3,1,0,2:T(2,128)(2,1)}), bf16[1,2,512,512]{3,1,0,2:T(2,128)(2,1)S(1)}, u32[]{:S(2)}, u32[]{:S(2)}) async-start(bf16[1,2,512,512]{3,1,0,2:T(2,128)(2,1)} %copy.32), calls=%async_computation | async-start | bytes 2097152 | tf_op jit(solution)/shard_map/all_to_all | solution.py:98
  7.5 0.7 fusion.82
  8.2 13.7 %all-to-all-done = bf16[1,2,512,512]{3,1,0,2:T(2,128)(2,1)S(1)} async-done(((bf16[1,2,512,512]{3,1,0,2:T(2,128)(2,1)}), bf16[1,2,512,512]{3,1,0,2:T(2,128)(2,1)S(1)}, u32[]{:S(2)}, u32[]{:S(2)}) %all-to-all-start) | async-done | bytes 1048608 | tf_op jit(solution)/shard_map/all_to_all | solution.py:98
  22.0 1.1 copy.50
  23.1 1.2 all_to_all.22
  24.4 1.9 collective-permute-start
  26.3 1.3 maximum_bitcast_fusion
  30.1 0.1 broadcast_multiply_fusion.3
  30.2 7.3 %collective-permute-done = bf16[1,2,128,1024]{3,2,1,0:T(8,128)(2,1)S(1)} collective-permute-done((bf16[1,2,128,1024]{3,2,1,0:T(8,128)(2,1)S(1)}, bf16[1,2,128,1024]{3,2,1,0:T(8,128)(2,1)S(1)}, u32[]{:S(2)}, u32[]{:S(2)}) %collective-permute-start) | collective-permute-done | bytes 524320 | tf_op jit(solution)/shard_map/ppermute | solution.py:12
  37.5 17.8 %fusion.29 = f32[2,1,2,128,1024]{4,3,2,0,1:T(8,128)S(1)} fusion(bf16[1,1,2,128,1024]{4,3,2,0,1:T(8,128)(2,1)S(1)} %bitcast.99, bf16[1,1,2,128,1024]{4,3,2,0,1:T(8,128)(2,1)S(1)} %get-tuple-element.15), kind=kOutput, calls=%fused_computation.40 | convolution fusion | flops 1097334784 | bytes 3145728 | tf_op jit(solution)/shard_map/dot_general | solution.py:49
  55.4 0.1 fusion.59
  55.5 8.0 %fusion.54 = (f32[2,1,1,128,1024]{4,3,2,0,1:T(8,128)S(1)}, f32[2,1,1,128,1024]{4,3,2,0,1:T(8,128)S(1)}, f32[2,1,1,128,1024]{4,3,2,0,1:T(8,128)S(1)}, f32[2,1,1,128,1024]{4,3,2,0,1:T(8,128)S(1)}) fusion(f32[2,1,2,128,1024]{4,3,2,0,1:T(8,128)S(1)} %fusion.59, f32[2]{0:T(128)S(1)} %maximum_bitcast_fusion, f32[128,1024]{1,0:T(8,128)S(1)} %get-tuple-element.29, ...), kind=kLoop, calls=%fused_computation.71 | loop fusion | flops 3670016 | bytes 9437192 | tf_op jit(solution)/shard_map/sub | solution.py:33
  63.5 0.1 maximum_reduce_fusion
  63.7 0.1 maximum_reduce_fusion.1
  63.9 0.8 copy.34
  64.7 0.6 constant_dynamic-slice_fusion.1
  65.4 1.1 copy.46
  66.5 2.6 %collective-permute-start.1 = (bf16[1,2,64,2048]{3,2,1,0:T(8,128)(2,1)}, bf16[1,2,64,2048]{3,2,1,0:T(8,128)(2,1)S(1)}, u32[]{:S(2)}, u32[]{:S(2)}) collective-permute-start(bf16[1,2,64,2048]{3,2,1,0:T(8,128)(2,1)} %copy.46), channel_id=1, source_target_pairs={{0,8},{4,12},{8,0},{12,4},{1,9},{5,13},{9,1},{13,5},{2,10},{6,14},... | collective-permute-start | bytes 1572872 | tf_op jit(solution)/shard_map/ppermute | solution.py:12
  69.2 0.2 broadcast_multiply_fusion.1
  69.4 0.3 copy.35
  69.7 21.4 %collective-permute-done.1 = bf16[1,2,64,2048]{3,2,1,0:T(8,128)(2,1)S(1)} collective-permute-done((bf16[1,2,64,2048]{3,2,1,0:T(8,128)(2,1)}, bf16[1,2,64,2048]{3,2,1,0:T(8,128)(2,1)S(1)}, u32[]{:S(2)}, u32[]{:S(2)}) %collective-permute-start.1) | collective-permute-done | bytes 524320 | tf_op jit(solution)/shard_map/ppermute | solution.py:12
  91.2 0.1 fusion.58
  91.3 72.2 %fusion.15 = f32[2,1,2,64,2048]{4,3,2,0,1:T(8,128)S(1)} fusion(bf16[2,2,64,2048]{3,2,1,0:T(8,128)(2,1)S(1)} %fusion.89), kind=kOutput, calls=%fused_computation.25 | convolution fusion | flops 2239758336 | bytes 3145728 | tf_op jit(solution)/shard_map/dot_general | solution.py:49
  163.5 8.0 %fusion.50 = (f32[2,1,1,64,2048]{4,3,2,0,1:T(8,128)S(1)}, f32[2,1,1,64,2048]{4,3,2,0,1:T(8,128)S(1)}, f32[2,1,1,64,2048]{4,3,2,0,1:T(8,128)S(1)}, f32[2,1,1,64,2048]{4,3,2,0,1:T(8,128)S(1)}) fusion(f32[2,1,2,64,2048]{4,3,2,0,1:T(8,128)S(1)} %fusion.58, f32[2]{0:T(128)S(1)} %maximum_bitcast_fusion.1, f32[64,2048]{1,0:T(8,128)S(1)} %get-tuple-element.19, ...), kind=kLoop, calls=%fused_computation.67 | loop fusion | flops 3670016 | bytes 9437192 | tf_op jit(solution)/shard_map/sub | solution.py:33
  171.5 0.1 maximum_reduce_fusion.2
  171.9 1.5 copy.37
  173.4 0.8 copy.38
  174.2 0.6 gather_fusion
  175.0 30.2 %all_to_all.28 = bf16[4,2,1,2,512,64]{4,5,3,2,1,0:T(8,128)(2,1)S(1)} all-to-all(bf16[4,2,1,2,512,64]{4,5,3,2,1,0:T(8,128)(2,1)S(1)} %bitcast.90), channel_id=1, replica_groups=mesh['swath'=2,'sub'=4,'beam'=2,'half'=2] {'sub'}, dimensions={0} | all-to-all | bytes 2097152 | tf_op jit(solution)/shard_map/all_to_all | solution.py:116
  205.2 15.6 %all_to_all.29 = bf16[4,2,1,2,512,64]{4,5,3,2,0,1:T(8,128)(2,1)S(1)} all-to-all(bf16[4,2,1,2,512,64]{4,5,3,2,0,1:T(8,128)(2,1)S(1)} %copy.40), channel_id=1, replica_groups=mesh['swath'=2,'sub'=4,'beam'=2,'half'=2] {'beam'}, dimensions={1} | all-to-all | bytes 2097152 | tf_op jit(solution)/shard_map/all_to_all | solution.py:115
  221.0 1.3 copy.43
  (20 shorter events, 1.1 us)
Async XLA Ops:
  0.0 7.5 %copy-start = (f32[4]{0:T(128)S(1)}, f32[4]{0:T(128)}, u32[]{:S(2)}) copy-start(f32[4]{0:T(128)} %param.4) | copy-start | bytes 52
  3.3 18.7 %all-to-all-start = ((bf16[1,2,512,512]{3,1,0,2:T(2,128)(2,1)}), bf16[1,2,512,512]{3,1,0,2:T(2,128)(2,1)S(1)}, u32[]{:S(2)}, u32[]{:S(2)}) async-start(bf16[1,2,512,512]{3,1,0,2:T(2,128)(2,1)} %copy.32), calls=%async_computation | async-start | bytes 2097152 | tf_op jit(solution)/shard_map/all_to_all | solution.py:98
  23.0 7.0 %copy-start.1 = (s32[2,4]{1,0:T(2,128)S(1)}, s32[2,4]{1,0:T(2,128)}, u32[]{:S(2)}) copy-start(s32[2,4]{1,0:T(2,128)} %param.5) | copy-start | bytes 100
  24.4 13.2 %collective-permute-start = (bf16[1,2,128,1024]{3,2,1,0:T(8,128)(2,1)S(1)}, bf16[1,2,128,1024]{3,2,1,0:T(8,128)(2,1)S(1)}, u32[]{:S(2)}, u32[]{:S(2)}) collective-permute-start(bf16[1,2,128,1024]{3,2,1,0:T(8,128)(2,1)S(1)} %get-tuple-element.16), channel_id=1, source_target_pairs={{0,4},{4,0},{8,12},{12,8},{1,5},{5,1},{9,13},{13,9},{2,6},{6,2},{1... | collective-permute-start | bytes 1572872 | tf_op jit(solution)/shard_map/ppermute | solution.py:12
  66.5 24.6 %collective-permute-start.1 = (bf16[1,2,64,2048]{3,2,1,0:T(8,128)(2,1)}, bf16[1,2,64,2048]{3,2,1,0:T(8,128)(2,1)S(1)}, u32[]{:S(2)}, u32[]{:S(2)}) collective-permute-start(bf16[1,2,64,2048]{3,2,1,0:T(8,128)(2,1)} %copy.46), channel_id=1, source_target_pairs={{0,8},{4,12},{8,0},{12,4},{1,9},{5,13},{9,1},{13,5},{2,10},{6,14},... | collective-permute-start | bytes 1572872 | tf_op jit(solution)/shard_map/ppermute | solution.py:12
where the time goes:
time: 226 us; the launch traced here: 223 us
  matrix products  90 us (40%)
  blocking collectives  45.8 us (20%)
  waiting for transfers between devices  42.4 us (19%)
  other arithmetic  18.8 us (8%)
  local copies, waits for them, and re-layouts  14 us (6%)
  starting transfers between devices  8.68 us (4%)
  between operations  2.96 us (1%)
    dot_general x2, matrix products, odd_local(): jnp.dot(children.reshape(-1, children.shape[-1]), kernel, preferred_eleme...  90 us
    all_to_all x1, blocking collectives, body(): lax.all_to_all(outgoing, 'sub', split_axis=0, concat_axis=0, tiled=True)  30.2 us
    ppermute x2, waiting for transfers between devices, swapped(): lax.ppermute(value, axis, [(i, i ^ 1 << distance) for i in range(lax.axis...  28.7 us
    sub x2, other arithmetic, steer_phase(): real_part * cosine - imag_part * sines  16 us
    all_to_all x1, blocking collectives, body(): lax.all_to_all(lax.all_to_all(outgoing, 'sub', split_axis=0, concat_axis=...  15.6 us
    all_to_all x1, waiting for transfers between devices, body(): lax.all_to_all(images, 'beam', split_axis=2, concat_axis=3, tiled=True)  13.7 us
  transfers between devices with their start and end apart: 3, of which 3 were waited for; matrix products, arithmetic and copies ran while one was open for 1% of the time, Pallas kernels for 0%

commit v1 on v0

--- a/solution.py
+++ b/solution.py
@@ -112,12 +112,20 @@
     beam_ids = jnp.arange(beam_count, dtype=jnp.int32)[:, None]
     picked = sector_tiles[:, :, :, beam_ids, owners, :]
     outgoing = picked.transpose(4, 3, 0, 1, 5, 2)
-    received = lax.all_to_all(
-        lax.all_to_all(outgoing, "sub", split_axis=0, concat_axis=0, tiled=True),
-        "beam",
-        split_axis=1,
-        concat_axis=1,
-        tiled=True,
+    received = jnp.concatenate(
+        lax.all_to_all(
+            jnp.stack(
+                jnp.split(
+                    lax.all_to_all(outgoing, "sub", split_axis=0, concat_axis=0, tiled=True),
+                    lax.axis_size("beam"),
+                    axis=1,
+                )
+            ),
+            "beam",
+            0,
+            0,
+        ),
+        axis=1,
     )
     sector_width = received.shape[4]
     received = received.reshape(

time: 226 us -> 226 us (level)
  no operation moved by 1% of the time
where the time goes in v1:
time: 226 us; the launch traced here: 223 us
  matrix products  90 us (40%)
  blocking collectives  45.8 us (20%)
  waiting for transfers between devices  42.4 us (19%)
  other arithmetic  19 us (8%)
  local copies, waits for them, and re-layouts  14 us (6%)
  starting transfers between devices  8.68 us (4%)
  between operations  2.92 us (1%)
    dot_general x2, matrix products, odd_local(): jnp.dot(children.reshape(-1, children.shape[-1]), kernel, preferred_eleme...  90 us
    all_to_all x1, blocking collectives, body(): lax.all_to_all(outgoing, 'sub', split_axis=0, concat_axis=0, tiled=True)  30.2 us
    ppermute x2, waiting for transfers between devices, swapped(): lax.ppermute(value, axis, [(i, i ^ 1 << distance) for i in range(lax.axis...  28.6 us
    sub x2, other arithmetic, steer_phase(): real_part * cosine - imag_part * sines  16 us
    all_to_all x1, blocking collectives, body(): lax.all_to_all(jnp.stack(jnp.split(lax.all_to_all(outgoing, 'sub', split_...  15.6 us
    all_to_all x1, waiting for transfers between devices, body(): lax.all_to_all(images, 'beam', split_axis=2, concat_axis=3, tiled=True)  13.7 us
  transfers between devices with their start and end apart: 3, of which 3 were waited for; matrix products, arithmetic and copies ran while one was open for 1% of the time, Pallas kernels for 0%

profile of v1, /device:TPU:0, one launch (start us, length us, event | category | flops | bytes accessed | tf_op | source)
XLA Modules:
  0.0 222.7 jit_solution(11036074471717078610)
XLA Ops:
  0.0 3.3 %copy.23 = bf16[1,2,512,512]{3,1,0,2:T(2,128)(2,1)} copy(bf16[1,2,512,512]{3,2,1,0:T(8,128)(2,1)} %param.3) | data formatting | bytes 2097152 | tf_op args[0]
  3.3 4.2 %all-to-all-start = ((bf16[1,2,512,512]{3,1,0,2:T(2,128)(2,1)}), bf16[1,2,512,512]{3,1,0,2:T(2,128)(2,1)S(1)}, u32[]{:S(2)}, u32[]{:S(2)}) async-start(bf16[1,2,512,512]{3,1,0,2:T(2,128)(2,1)} %copy.23), calls=%async_computation | async-start | bytes 2097152 | tf_op jit(solution)/shard_map/all_to_all | solution.py:98
  7.5 0.7 fusion.82
  8.3 13.7 %all-to-all-done = bf16[1,2,512,512]{3,1,0,2:T(2,128)(2,1)S(1)} async-done(((bf16[1,2,512,512]{3,1,0,2:T(2,128)(2,1)}), bf16[1,2,512,512]{3,1,0,2:T(2,128)(2,1)S(1)}, u32[]{:S(2)}, u32[]{:S(2)}) %all-to-all-start) | async-done | bytes 1048608 | tf_op jit(solution)/shard_map/all_to_all | solution.py:98
  22.0 1.1 copy.43
  23.1 1.2 all_to_all.22
  24.4 1.9 collective-permute-start
  26.3 1.4 maximum_bitcast_fusion.1
  30.1 0.1 broadcast_multiply_fusion.3
  30.3 7.3 %collective-permute-done = bf16[1,2,128,1024]{3,2,1,0:T(8,128)(2,1)S(1)} collective-permute-done((bf16[1,2,128,1024]{3,2,1,0:T(8,128)(2,1)S(1)}, bf16[1,2,128,1024]{3,2,1,0:T(8,128)(2,1)S(1)}, u32[]{:S(2)}, u32[]{:S(2)}) %collective-permute-start) | collective-permute-done | bytes 524320 | tf_op jit(solution)/shard_map/ppermute | solution.py:12
  37.5 17.8 %fusion.29 = f32[2,1,2,128,1024]{4,3,2,0,1:T(8,128)S(1)} fusion(bf16[1,1,2,128,1024]{4,3,2,0,1:T(8,128)(2,1)S(1)} %bitcast.109, bf16[1,1,2,128,1024]{4,3,2,0,1:T(8,128)(2,1)S(1)} %get-tuple-element.17), kind=kOutput, calls=%fused_computation.40 | convolution fusion | flops 1097334784 | bytes 3145728 | tf_op jit(solution)/shard_map/dot_general | solution.py:49
  55.4 0.1 fusion.59
  55.5 8.0 %fusion.54 = (f32[2,1,1,128,1024]{4,3,2,0,1:T(8,128)S(1)}, f32[2,1,1,128,1024]{4,3,2,0,1:T(8,128)S(1)}, f32[2,1,1,128,1024]{4,3,2,0,1:T(8,128)S(1)}, f32[2,1,1,128,1024]{4,3,2,0,1:T(8,128)S(1)}) fusion(f32[2,1,2,128,1024]{4,3,2,0,1:T(8,128)S(1)} %fusion.59, f32[2]{0:T(128)S(1)} %maximum_bitcast_fusion.1, f32[128,1024]{1,0:T(8,128)S(1)} %get-tuple-element.31, ...), kind=kLoop, calls=%fused_computation.71 | loop fusion | flops 3670016 | bytes 9437192 | tf_op jit(solution)/shard_map/sub | solution.py:33
  63.5 0.1 maximum_reduce_fusion
  63.7 0.1 maximum_reduce_fusion.1
  63.9 0.8 copy.25
  64.7 0.6 constant_dynamic-slice_fusion.1
  65.4 1.1 copy.38
  66.5 2.6 %collective-permute-start.1 = (bf16[1,2,64,2048]{3,2,1,0:T(8,128)(2,1)}, bf16[1,2,64,2048]{3,2,1,0:T(8,128)(2,1)S(1)}, u32[]{:S(2)}, u32[]{:S(2)}) collective-permute-start(bf16[1,2,64,2048]{3,2,1,0:T(8,128)(2,1)} %copy.38), channel_id=1, source_target_pairs={{0,8},{4,12},{8,0},{12,4},{1,9},{5,13},{9,1},{13,5},{2,10},{6,14},... | collective-permute-start | bytes 1572872 | tf_op jit(solution)/shard_map/ppermute | solution.py:12
  69.2 0.2 broadcast_multiply_fusion.1
  69.4 0.3 copy.26
  69.7 21.4 %collective-permute-done.1 = bf16[1,2,64,2048]{3,2,1,0:T(8,128)(2,1)S(1)} collective-permute-done((bf16[1,2,64,2048]{3,2,1,0:T(8,128)(2,1)}, bf16[1,2,64,2048]{3,2,1,0:T(8,128)(2,1)S(1)}, u32[]{:S(2)}, u32[]{:S(2)}) %collective-permute-start.1) | collective-permute-done | bytes 524320 | tf_op jit(solution)/shard_map/ppermute | solution.py:12
  91.2 0.1 fusion.58
  91.3 72.2 %fusion.15 = f32[2,1,2,64,2048]{4,3,2,0,1:T(8,128)S(1)} fusion(bf16[2,2,64,2048]{3,2,1,0:T(8,128)(2,1)S(1)} %fusion.89), kind=kOutput, calls=%fused_computation.25 | convolution fusion | flops 2239758336 | bytes 3145728 | tf_op jit(solution)/shard_map/dot_general | solution.py:49
  163.5 8.0 %fusion.50 = (f32[2,1,1,64,2048]{4,3,2,0,1:T(8,128)S(1)}, f32[2,1,1,64,2048]{4,3,2,0,1:T(8,128)S(1)}, f32[2,1,1,64,2048]{4,3,2,0,1:T(8,128)S(1)}, f32[2,1,1,64,2048]{4,3,2,0,1:T(8,128)S(1)}) fusion(f32[2,1,2,64,2048]{4,3,2,0,1:T(8,128)S(1)} %fusion.58, f32[2]{0:T(128)S(1)} %maximum_bitcast_fusion.2, f32[64,2048]{1,0:T(8,128)S(1)} %get-tuple-element.21, ...), kind=kLoop, calls=%fused_computation.67 | loop fusion | flops 3670016 | bytes 9437192 | tf_op jit(solution)/shard_map/sub | solution.py:33
  171.5 0.1 maximum_reduce_fusion.2
  171.9 1.5 copy.28
  173.4 0.8 copy.29
  174.2 0.6 gather_fusion
  175.0 30.2 %all_to_all.28 = bf16[4,2,1,2,512,64]{4,5,3,2,1,0:T(8,128)(2,1)S(1)} all-to-all(bf16[4,2,1,2,512,64]{4,5,3,2,1,0:T(8,128)(2,1)S(1)} %bitcast.100), channel_id=1, replica_groups=mesh['swath'=2,'sub'=4,'beam'=2,'half'=2] {'sub'}, dimensions={0} | all-to-all | bytes 2097152 | tf_op jit(solution)/shard_map/all_to_all | solution.py:119
  205.3 15.6 %all_to_all.29 = bf16[2,4,1,1,2,512,64]{5,6,4,3,2,1,0:T(8,128)(2,1)S(1)} all-to-all(bf16[2,4,1,1,2,512,64]{5,6,4,3,2,1,0:T(8,128)(2,1)S(1)} %maximum_bitcast_fusion), channel_id=1, replica_groups=mesh['swath'=2,'sub'=4,'beam'=2,'half'=2] {'beam'}, dimensions={0} | all-to-all | bytes 2097152 | tf_op jit(solution)/shard_map/all_to_all | solution.py:116
  221.1 1.3 copy.35
  (21 shorter events, 1.2 us)
Async XLA Ops:
  0.0 7.5 %copy-start = (f32[4]{0:T(128)S(1)}, f32[4]{0:T(128)}, u32[]{:S(2)}) copy-start(f32[4]{0:T(128)} %param.4) | copy-start | bytes 52
  3.3 18.7 %all-to-all-start = ((bf16[1,2,512,512]{3,1,0,2:T(2,128)(2,1)}), bf16[1,2,512,512]{3,1,0,2:T(2,128)(2,1)S(1)}, u32[]{:S(2)}, u32[]{:S(2)}) async-start(bf16[1,2,512,512]{3,1,0,2:T(2,128)(2,1)} %copy.23), calls=%async_computation | async-start | bytes 2097152 | tf_op jit(solution)/shard_map/all_to_all | solution.py:98
  23.0 7.0 %copy-start.1 = (s32[2,4]{1,0:T(2,128)S(1)}, s32[2,4]{1,0:T(2,128)}, u32[]{:S(2)}) copy-start(s32[2,4]{1,0:T(2,128)} %param.5) | copy-start | bytes 100
  24.4 13.2 %collective-permute-start = (bf16[1,2,128,1024]{3,2,1,0:T(8,128)(2,1)S(1)}, bf16[1,2,128,1024]{3,2,1,0:T(8,128)(2,1)S(1)}, u32[]{:S(2)}, u32[]{:S(2)}) collective-permute-start(bf16[1,2,128,1024]{3,2,1,0:T(8,128)(2,1)S(1)} %get-tuple-element.18), channel_id=1, source_target_pairs={{0,4},{4,0},{8,12},{12,8},{1,5},{5,1},{9,13},{13,9},{2,6},{6,2},{1... | collective-permute-start | bytes 1572872 | tf_op jit(solution)/shard_map/ppermute | solution.py:12
  66.5 24.6 %collective-permute-start.1 = (bf16[1,2,64,2048]{3,2,1,0:T(8,128)(2,1)}, bf16[1,2,64,2048]{3,2,1,0:T(8,128)(2,1)S(1)}, u32[]{:S(2)}, u32[]{:S(2)}) collective-permute-start(bf16[1,2,64,2048]{3,2,1,0:T(8,128)(2,1)} %copy.38), channel_id=1, source_target_pairs={{0,8},{4,12},{8,0},{12,4},{1,9},{5,13},{9,1},{13,5},{2,10},{6,14},... | collective-permute-start | bytes 1572872 | tf_op jit(solution)/shard_map/ppermute | solution.py:12
